TPU v7x, 256 devices: a whole 4x4x8 slice. The times are simulated.
256 devices in a mesh: group: 16 (over y_hi, x, core), leaf: 16 (over y_lo, z).
Axes of the slice: x: 4, y: 4 (y_hi: 2, y_lo: 2; y = y_hi * 2 + y_lo), z: 8, core: 2. Of those that a mesh axis runs over, the one named last changes fastest.
Arguments:
- leaf_mass: bfloat16 [256, 512, 512], P(('group', 'leaf')), may hold values from -23 to 23, as said below
- leaf_damp: bfloat16 [256, 512, 512], P(('group', 'leaf')), may hold values from -12 to 12, as said below
- mass_coupling: bfloat16 [256, 512, 1536], P(('group', 'leaf')), may hold values from -6 to 6
- damp_coupling: bfloat16 [256, 512, 1536], P(('group', 'leaf')), may hold values from -6 to 6
- leaf_modes: bfloat16 [256, 512, 1536], P(('group', 'leaf')), may hold values from -0.15625 to 0.15625
- interface_blocks: int32 [256, 12], P(('group', 'leaf')), may hold values from 0 to 11, each once within a row
- mid_modes: bfloat16 [16, 1536, 256], P('group', 'leaf'), may hold values from -0.15625 to 0.15625
- mid_constraint: bfloat16 [16, 1536, 1024], P('group', 'leaf'), may hold values from -0.109375 to 0.109375
Outputs:
- coupling_mass: float32 [256, 512, 256], P(('group', 'leaf'))
- coupling_damp: float32 [256, 512, 256], P(('group', 'leaf'))
- modal_mass: float32 [16, 256, 1280], P('group', 'leaf')
- modal_damp: float32 [16, 256, 1280], P('group', 'leaf')
- root_mass: float32 [1024, 1024], P(('group', 'leaf'))
- root_damp: float32 [1024, 1024], P(('group', 'leaf'))
Inputs may be any that keep to these rules, and one draw needn't show every extreme that they name: `interface_blocks`: each row is a permutation of 0 to 11. `leaf_mass`: each leaf's block is symmetric. `leaf_damp`: each leaf's block is symmetric.
All inputs are finite; a program needn't handle non-finite values.
Results may differ from a plain program's by a relative error of at most 0.0049.
Values may be sent and summed in bfloat16 or wider, within the bound.
No kernel may reach another device: no remote copies, remote signals or barrier semaphores. Data moves between devices by JAX's collectives and lax.ppermute only.
A program may use at most 128 MiB of HBM per device.

v0:
```python
import jax
import jax.numpy as jnp
from jax import lax
from jax.sharding import PartitionSpec as P


def to_middle(stacked, onehot, block_count, block_size):
    rows_total, width_total = stacked.shape
    moved = jnp.einsum(
        "lbk,bj->ljk",
        stacked.reshape(rows_total, block_count, block_size),
        onehot,
        preferred_element_type=jnp.float32,
    )
    return moved.astype(jnp.bfloat16).reshape(rows_total, width_total)


def left_product(first_operand, second_operand):
    return lax.dot_general(
        first_operand, second_operand, (((0,), (0,)), ((), ())), preferred_element_type=jnp.float32
    )


def body(
    leaf_mass,
    leaf_damp,
    mass_coupling,
    damp_coupling,
    leaf_modes,
    interface_blocks,
    mid_modes,
    mid_constraint,
):
    leaf_order = leaf_mass.shape[1]
    block_count = interface_blocks.shape[1]
    sep_width = leaf_modes.shape[2]
    block_size = sep_width // block_count
    mode_count = mid_modes.shape[2]
    root_width = mid_constraint.shape[2]
    basis_width = mode_count + root_width
    leaf_count = lax.axis_size("leaf")
    group_count = lax.axis_size("group")
    onehot = (
        interface_blocks[0][:, None] == jnp.arange(block_count, dtype=jnp.int32)[None, :]
    ).astype(jnp.bfloat16)
    placed = to_middle(
        jnp.concatenate([leaf_modes[0], mass_coupling[0], damp_coupling[0]], axis=0),
        onehot,
        block_count,
        block_size,
    )
    constraint = placed[:leaf_order]
    sides = placed[leaf_order:].astype(jnp.float32)
    product = jnp.dot(
        jnp.concatenate([leaf_mass[0], leaf_damp[0]], axis=0),
        constraint,
        preferred_element_type=jnp.float32,
    )
    half_work = (0.5 * product + sides).astype(jnp.bfloat16)
    full_work = (product + sides).astype(jnp.bfloat16)
    basis_rows = jnp.concatenate([mid_modes[0], mid_constraint[0]], axis=1)
    mode_basis = lax.all_gather(basis_rows, "leaf", axis=0, tiled=True)
    left_sum = jnp.dot(constraint, mode_basis, preferred_element_type=jnp.float32)
    right_sum = jnp.dot(half_work, mode_basis, preferred_element_type=jnp.float32)
    coupling = jnp.dot(full_work, mode_basis[:, :mode_count], preferred_element_type=jnp.float32)
    left_part = left_sum.astype(jnp.bfloat16)
    right_part = right_sum.astype(jnp.bfloat16)
    right_mass = right_part[:leaf_order]
    right_damp = right_part[leaf_order:]

    def projected_rows(first_row, amount, first_col):
        left_rows = lax.dynamic_slice_in_dim(left_part, first_row, amount, 1)
        right_rows = lax.dynamic_slice_in_dim(right_part, first_row, amount, 1)
        left_cols = left_part[:, first_col:]
        mass_term = left_product(left_rows, right_mass[:, first_col:]) + left_product(
            right_rows[:leaf_order], left_cols
        )
        damp_term = left_product(left_rows, right_damp[:, first_col:]) + left_product(
            right_rows[leaf_order:], left_cols
        )
        return jnp.concatenate([mass_term, damp_term], axis=1)

    modal_part = lax.psum_scatter(
        projected_rows(jnp.int32(0), mode_count, 0), "leaf", scatter_dimension=0, tiled=True
    )
    device_count = group_count * leaf_count
    core_odd = lax.axis_index("group") % 2 == 1
    left_root = left_part[:, mode_count:]
    mass_root = right_mass[:, mode_count:]
    damp_root = right_damp[:, mode_count:]
    own_right = jnp.where(core_odd, damp_root, mass_root)
    other_right = jnp.where(core_odd, mass_root, damp_root)
    partner = lax.ppermute(
        jnp.concatenate([left_root, other_right], axis=0),
        "group",
        [(index, index ^ 1) for index in range(group_count)],
    )
    left_pair = jnp.concatenate([left_root, partner[:leaf_order]], axis=0)
    right_pair = jnp.concatenate([own_right, partner[leaf_order:]], axis=0)
    root_rows = left_product(left_pair, right_pair) + left_product(right_pair, left_pair)
    root_recv = lax.all_to_all(
        root_rows.reshape(device_count, root_width // device_count, root_width).astype(
            jnp.bfloat16
        ),
        ("group", "leaf"),
        0,
        0,
        tiled=True,
    )
    root_part = jnp.sum(
        root_recv.reshape(
            group_count // 2, 2, leaf_count, root_width // device_count, root_width
        ).astype(jnp.float32),
        axis=(0, 2),
    )
    return (
        coupling[:leaf_order][None],
        coupling[leaf_order:][None],
        modal_part[:, :basis_width][None],
        modal_part[:, basis_width:][None],
        root_part[0],
        root_part[1],
    )


def solution(mesh):
    return jax.shard_map(
        body,
        mesh=mesh,
        in_specs=(
            P(("group", "leaf"), None, None),
            P(("group", "leaf"), None, None),
            P(("group", "leaf"), None, None),
            P(("group", "leaf"), None, None),
            P(("group", "leaf"), None, None),
            P(("group", "leaf"), None),
            P("group", "leaf", None),
            P("group", "leaf", None),
        ),
        out_specs=(
            P(("group", "leaf"), None, None),
            P(("group", "leaf"), None, None),
            P("group", "leaf", None),
            P("group", "leaf", None),
            P(("group", "leaf"), None),
            P(("group", "leaf"), None),
        ),
        check_vma=False,
    )
```

profile of v0, /device:TPU:4, one launch (start us, length us, event | category | flops | bytes accessed | tf_op | source)
XLA Modules:
  0.0 214.4 jit_solution(18022343488197545717)
XLA Ops:
  7.2 0.0 all-gather.2.cloned.1.call-start
  7.2 1.6 pad_maximum_fusion.8
  8.9 0.0 all-gather.2.cloned.1.call-update
  8.9 0.0 reduce-scatter.2.cloned.1.call-start
  8.9 1.7 copy.26
  10.7 0.0 copy-start.3
  10.7 3.0 %copy.29 = bf16[512,12,128]{2,1,0:T(8,128)(2,1)} copy(bf16[512,12,128]{0,2,1:T(8,128)(2,1)S(1)} %bitcast.40) | data formatting | bytes 3145728 | tf_op jit(solution)/shard_map/concatenate | solution.py:47
  13.7 0.7 copy.25
  14.4 0.0 copy-start.4
  14.4 3.0 %copy.28 = bf16[512,12,128]{2,1,0:T(8,128)(2,1)} copy(bf16[512,12,128]{0,2,1:T(8,128)(2,1)S(1)} %bitcast.41) | data formatting | bytes 3145728 | tf_op jit(solution)/shard_map/concatenate | solution.py:47
  17.5 0.7 copy.24
  18.2 0.0 copy-start.8
  18.2 3.0 %copy.27 = bf16[512,12,128]{2,1,0:T(8,128)(2,1)} copy(bf16[512,12,128]{0,2,1:T(8,128)(2,1)S(1)} %bitcast.42) | data formatting | bytes 3145728 | tf_op jit(solution)/shard_map/concatenate | solution.py:47
  21.2 4.6 %fusion = bf16[12,1536,128]{2,0,1:T(8,128)(2,1)S(1)} fusion(bf16[512,12,128]{2,1,0:T(8,128)(2,1)} %copy.29, bf16[512,12,128]{2,1,0:T(8,128)(2,1)} %copy.28, bf16[512,12,128]{2,1,0:T(8,128)(2,1)} %copy.27, s32[12]{0:T(128)S(1)} %bitcast.49), kind=kOutput, calls=%fused_computation.1 | convolution fusion | flops 70779024 | bytes 9437232 | tf_op jit(solution)/shard_map/lbk,bj->ljk/dot_general | solution.py:9
  25.8 1.2 copy.38
  27.1 2.2 %copy-done.1 = bf16[12,1536,128]{2,1,0:T(8,128)(2,1)} copy-done((bf16[12,1536,128]{2,1,0:T(8,128)(2,1)}, bf16[12,1536,128]{2,1,0:T(8,128)(2,1)S(1)}, u32[]{:S(2)}) %copy-start.1) | copy-done | bytes 4718616
  29.3 0.1 slice.81
  29.4 0.7 copy.31
  30.1 5.1 %slice_convert_fusion = f32[1024,12,128]{2,0,1:T(8,128)} fusion(bf16[1536,12,128]{2,0,1:T(8,128)(2,1)} %bitcast.38), kind=kLoop, calls=%fused_computation.14 | loop fusion | flops 1572864 | bytes 9437184 | tf_op jit(solution)/shard_map/convert_element_type | solution.py:53
  35.3 6.6 %copy.32 = f32[1024,12,128]{0,2,1:T(8,128)} copy(f32[1024,12,128]{2,0,1:T(8,128)} %slice_convert_fusion) | data formatting | bytes 12582912 | tf_op jit(solution)/shard_map/convert_element_type | solution.py:53
  41.9 6.7 %copy.33 = f32[1024,1536]{1,0:T(8,128)} copy(f32[1024,1536]{0,1:T(8,128)} %bitcast.36) | data formatting | bytes 12582912 | tf_op jit(solution)/shard_map/convert_element_type | solution.py:53
  48.6 4.5 %fusion.14 = f32[1024,1536]{1,0:T(8,128)} fusion(bf16[512,1536]{0,1:T(8,128)(2,1)S(1)} %bitcast.43, bf16[512,512]{1,0:T(8,128)(2,1)S(1)} %bitcast.47, bf16[512,512]{1,0:T(8,128)(2,1)S(1)} %bitcast.48), kind=kOutput, calls=%fused_computation.28 | convolution fusion | flops 1612709888 | bytes 8912896 | tf_op jit(solution)/shard_map/dot_general | solution.py:54
  53.0 35.5 %all-gather.2.cloned.1.call-done = bf16[1536,1280]{1,0:T(8,128)(2,1)} async-done(((bf16[96,1280]{1,0:T(8,128)(2,1)}), bf16[1536,1280]{1,0:T(8,128)(2,1)}) %all-gather.2.cloned.1.call-update) | async-done | bytes 3932176 | tf_op jit(solution)/shard_map/all_gather | solution.py:62
  88.6 4.5 %convolution_convert_fusion.1 = bf16[512,1280]{1,0:T(8,128)(2,1)S(1)} fusion(bf16[512,1536]{0,1:T(8,128)(2,1)S(1)} %bitcast.44, bf16[1536,1280]{1,0:T(8,128)(2,1)} %all-gather.2.cloned.1.call-done), kind=kOutput, calls=%fused_computation.16 | convolution fusion | flops 2013921280 | bytes 6815744 | tf_op jit(solution)/shard_map/dot_general | solution.py:63
  93.1 0.1 slice.92
  93.2 1.1 copy-done.2
  94.3 6.6 %convolution_convert_fusion = bf16[1024,1280]{1,0:T(8,128)(2,1)S(1)} fusion(bf16[1536,1280]{1,0:T(8,128)(2,1)} %all-gather.2.cloned.1.call-done, f32[1024,1536]{1,0:T(8,128)S(1)} %copy-done, f32[1024,1536]{1,0:T(8,128)S(1)} %copy-done.2), kind=kOutput, calls=%fused_computation.12 | convolution fusion | flops 4032561152 | bytes 19136512 | tf_op jit(solution)/shard_map/dot_general | solution.py:64
  100.9 1.2 broadcast_select_fusion
  102.1 1.6 pad_maximum_fusion.1
  103.7 0.5 fusion.10
  104.2 0.5 fusion.12
  104.8 0.5 convolution_add_fusion
  105.3 0.5 convolution_add_fusion.1
  105.8 1.8 pad_maximum_fusion
  107.6 0.0 reduce-scatter.2.cloned.1.call-update
  107.7 0.4 collective-permute-done
  108.1 0.2 fusion.31
  108.3 0.6 copy-done.5
  108.9 2.4 %fusion.9 = f32[1024,1024]{1,0:T(8,128)S(1)} fusion(bf16[512,1024]{1,0:T(8,128)(2,1)S(1)} %get-tuple-element.9, bf16[512,1024]{1,0:T(8,128)(2,1)S(1)} %copy-done.5, bf16[512,1024]{1,0:T(8,128)(2,1)S(1)} %slice.92, bf16[512,1024]{1,0:T(8,128)(2,1)S(1)} %get-tuple-element.8), kind=kOutput, calls=%fused_computation.23 | convolution fusion | flops 2155872256 | bytes 8388608 | tf_op jit(solution)/shard_map/dot_general | solution.py:19
  111.3 2.6 %add_convert_fusion.2 = bf16[1024,1024]{1,0:T(8,128)(2,1)S(1)} fusion(f32[1024,1024]{1,0:T(8,128)S(1)} %fusion.9, bf16[512,1024]{1,0:T(8,128)(2,1)S(1)} %get-tuple-element.9, bf16[512,1024]{1,0:T(8,128)(2,1)S(1)} %copy-done.5, bf16[512,1024]{1,0:T(8,128)(2,1)S(1)} %slice.92, bf16[512,1024]{1,0:T(8,128)(2,1)S(1)} %get-tuple-element.8), kind=kOutput, calls=%fused_computation.11 | convolution fusion | flops 2157969408 | bytes 10485760 | tf_op jit(solution)/shard_map/dot_general | solution.py:19
  113.9 2.2 %convert_element_type.46 = bf16[256,4,1024]{2,1,0:T(4,128)(2,1)} reshape(bf16[1024,1024]{1,0:T(8,128)(2,1)S(1)} %add_convert_fusion.2) | data formatting | bytes 4194304 | tf_op jit(solution)/shard_map/convert_element_type | solution.py:102
  116.1 9.8 %all-to-all-start = ((bf16[256,4,1024]{2,1,0:T(4,128)(2,1)}), bf16[256,4,1024]{2,1,0:T(4,128)(2,1)S(1)}, u32[]{:S(2)}, u32[]{:S(2)}) async-start(bf16[256,4,1024]{2,1,0:T(4,128)(2,1)} %convert_element_type.46), calls=%async_computation.1 | async-start | bytes 4194304 | tf_op jit(solution)/shard_map/all_to_all | solution.py:101
  125.9 5.8 %fusion.7 = f32[1024,256]{1,0:T(8,128)S(1)} fusion(f32[1024,1536]{1,0:T(8,128)} %fusion.14, f32[1024,1536]{1,0:T(8,128)} %copy.33, bf16[1536,1280]{1,0:T(8,128)(2,1)} %all-gather.2.cloned.1.call-done), kind=kOutput, calls=%fused_computation.13 | convolution fusion | flops 808452096 | bytes 14417920 | tf_op jit(solution)/shard_map/dot_general | solution.py:65
  131.7 1.0 slice_bitcast_fusion
  132.8 71.7 %reduce-scatter.2.cloned.1.call-done = f32[16,2560]{1,0:T(8,128)} async-done(((f32[256,2560]{1,0:T(8,128)}), f32[16,2560]{1,0:T(8,128)}) %reduce-scatter.2.cloned.1.call-update) | async-done | bytes 163856 | tf_op jit(solution)/shard_map/reduce_scatter | solution.py:83
  204.5 1.6 slice_bitcast_fusion.2
  206.1 0.8 convert_reduce_fusion
  206.9 0.6 slice_bitcast_fusion.4
  (14 shorter events, 0.0 us)
Async XLA Ops:
  7.2 81.4 %all-gather.2.cloned.1.call-start = ((), (), s32[]{:S(2)}) async-start(), calls=%async_computation.2 | async-start | bytes 4177920 | tf_op jit(solution)/shard_map/all_gather | solution.py:62
  8.9 195.6 %reduce-scatter.2.cloned.1.call-start = ((), (), s32[]{:S(2)}) async-start(), calls=%async_computation.3 | async-start | bytes 2785280 | tf_op jit(solution)/shard_map/reduce_scatter | solution.py:83
  10.7 3.0 %copy-start.3 = (bf16[1,512,1536]{2,1,0:T(8,128)(2,1)S(1)}, bf16[1,512,1536]{2,1,0:T(8,128)(2,1)}, u32[]{:S(2)}) copy-start(bf16[1,512,1536]{2,1,0:T(8,128)(2,1)} %param.10) | copy-start | bytes 4718596
  14.4 3.0 %copy-start.4 = (bf16[1,512,1536]{2,1,0:T(8,128)(2,1)S(1)}, bf16[1,512,1536]{2,1,0:T(8,128)(2,1)}, u32[]{:S(2)}) copy-start(bf16[1,512,1536]{2,1,0:T(8,128)(2,1)} %param.12) | copy-start | bytes 4718596
  18.2 3.0 %copy-start.8 = (s32[1,12]{1,0:T(1,128)S(1)}, s32[1,12]{1,0:T(1,128)}, u32[]{:S(2)}) copy-start(s32[1,12]{1,0:T(1,128)} %param.13) | copy-start | bytes 148
  27.1 2.2 %copy-start.1 = (bf16[12,1536,128]{2,1,0:T(8,128)(2,1)}, bf16[12,1536,128]{2,1,0:T(8,128)(2,1)S(1)}, u32[]{:S(2)}) copy-start(bf16[12,1536,128]{2,1,0:T(8,128)(2,1)S(1)} %copy.38) | copy-start | bytes 14155780
  41.9 6.7 %copy-start.6 = (bf16[1,512,512]{2,1,0:T(8,128)(2,1)S(1)}, bf16[1,512,512]{2,1,0:T(8,128)(2,1)}, u32[]{:S(2)}) copy-start(bf16[1,512,512]{2,1,0:T(8,128)(2,1)} %param.9) | copy-start | bytes 1572868
  41.9 6.7 %copy-start.7 = (bf16[1,512,512]{2,1,0:T(8,128)(2,1)S(1)}, bf16[1,512,512]{2,1,0:T(8,128)(2,1)}, u32[]{:S(2)}) copy-start(bf16[1,512,512]{2,1,0:T(8,128)(2,1)} %param.8) | copy-start | bytes 1572868
  88.5 4.7 %copy-start = (f32[1024,1536]{1,0:T(8,128)S(1)}, f32[1024,1536]{1,0:T(8,128)}, u32[]{:S(2)}) copy-start(f32[1024,1536]{1,0:T(8,128)} %copy.33) | copy-start | bytes 18874372
  88.5 5.8 %copy-start.2 = (f32[1024,1536]{1,0:T(8,128)S(1)}, f32[1024,1536]{1,0:T(8,128)}, u32[]{:S(2)}) copy-start(f32[1024,1536]{1,0:T(8,128)} %fusion.14) | copy-start | bytes 18874372
  103.7 4.4 %collective-permute-start = (bf16[1024,1024]{1,0:T(8,128)(2,1)}, bf16[1024,1024]{1,0:T(8,128)(2,1)S(1)}, u32[]{:S(2)}, u32[]{:S(2)}) collective-permute-start(bf16[1024,1024]{1,0:T(8,128)(2,1)} %pad_maximum_fusion.1), channel_id=1, source_target_pairs={{0,16},{16,0},{32,48},{48,32},{64,80},{80,64},{96,112},{112,96},{1... | collective-permute-start | bytes 6291464 | tf_op jit(solution)/shard_map/ppermute | solution.py:93
  107.7 1.2 copy-start.5
  116.1 90.0 %all-to-all-start = ((bf16[256,4,1024]{2,1,0:T(4,128)(2,1)}), bf16[256,4,1024]{2,1,0:T(4,128)(2,1)S(1)}, u32[]{:S(2)}, u32[]{:S(2)}) async-start(bf16[256,4,1024]{2,1,0:T(4,128)(2,1)} %convert_element_type.46), calls=%async_computation.1 | async-start | bytes 4194304 | tf_op jit(solution)/shard_map/all_to_all | solution.py:101
Sparse Core Ops, SparseCore 0:
  10.3 78.1 all-gather.1
  107.8 96.6 reduce-scatter.1
where the time goes:
time: 215 us; the launch traced here: 214 us
  waiting for transfers between devices  108 us (50%)
  local copies, waits for them, and re-layouts  37.3 us (17%)
  matrix products  33.1 us (15%)
  between operations  14.2 us (7%)
  other arithmetic  12.2 us (6%)
  starting transfers between devices  9.88 us (5%)
    reduce_scatter x1, waiting for transfers between devices, body(): lax.psum_scatter(projected_rows(jnp.int32(0), mode_count, 0), 'leaf', sca...  71.7 us
    all_gather x1, waiting for transfers between devices, body(): mode_basis = lax.all_gather(basis_rows, 'leaf', axis=0, tiled=True)  35.5 us
    convert_element_type x2, local copies, waits for them, and re-layouts, body(): sides = placed[leaf_order:].astype(jnp.float32)  13.3 us
    all_to_all x1, starting transfers between devices, body(): lax.all_to_all(root_rows.reshape(device_count, root_width // device_count...  9.79 us
    concatenate x3, local copies, waits for them, and re-layouts, body(): jnp.concatenate([leaf_modes[0], mass_coupling[0], damp_coupling[0]], axis=0)  9.08 us
    dot_general x6, matrix products, left_product(): lax.dot_general(first_operand, second_operand, (((0,), (0,)), ((), ())),...  7.12 us
    unnamed x21, local copies, waits for them, and re-layouts  7.11 us
    dot_general x1, matrix products, body(): jnp.dot(half_work, mode_basis, preferred_element_type=jnp.float32)  6.6 us
  transfers between devices with their start and end apart: 4, of which 3 were waited for; matrix products, arithmetic and copies ran while one was open for 29% of the time, Pallas kernels for 0%

commit v1 on v0

--- a/solution.py
+++ b/solution.py
@@ -1,7 +1,23 @@
+import functools
 import jax
 import jax.numpy as jnp
 from jax import lax
 from jax.sharding import PartitionSpec as P
+
+
+def pack_results(base_x, mesh_ax):
+    return jnp.concatenate(
+        lax.all_to_all(
+            jnp.stack([base_x] * lax.axis_size(mesh_ax), 0),
+            axis_name=mesh_ax,
+            split_axis=0,
+            concat_axis=0,
+        ),
+        0,
+    )
+
+
+drive_the_scales = functools.partial(pack_results, mesh_ax="leaf")
 
 
 def to_middle(stacked, onehot, block_count, block_size):
@@ -59,7 +75,7 @@
     half_work = (0.5 * product + sides).astype(jnp.bfloat16)
     full_work = (product + sides).astype(jnp.bfloat16)
     basis_rows = jnp.concatenate([mid_modes[0], mid_constraint[0]], axis=1)
-    mode_basis = lax.all_gather(basis_rows, "leaf", axis=0, tiled=True)
+    mode_basis = drive_the_scales(basis_rows)
     left_sum = jnp.dot(constraint, mode_basis, preferred_element_type=jnp.float32)
     right_sum = jnp.dot(half_work, mode_basis, preferred_element_type=jnp.float32)
     coupling = jnp.dot(full_work, mode_basis[:, :mode_count], preferred_element_type=jnp.float32)

time: 215 us -> 239 us (1.11)
  starting transfers between devices: 9.88 us -> 22.3 us
  waiting for transfers between devices: 108 us -> 116 us
    all_to_all x0 -> x1, waiting for transfers between devices: none -> 44.2 us  [pack_results(): lax.all_to_all(jnp.stack([base_x] * lax.axis_size(mesh_ax), 0), axis_name...]
    all_gather x1 -> x0, waiting for transfers between devices: 35.5 us -> none  [body(): mode_basis = lax.all_gather(basis_rows, 'leaf', axis=0, tiled=True)]
    all_to_all x0 -> x1, starting transfers between devices: none -> 9.76 us  [pack_results(): lax.all_to_all(jnp.stack([base_x] * lax.axis_size(mesh_ax), 0), axis_name...]
    all_to_all x1, starting transfers between devices: 9.79 us -> 12.5 us  [body(): lax.all_to_all(root_rows.reshape(device_count, root_width // device_count...]
    unnamed x21 -> x25, local copies, waits for them, and re-layouts: 7.11 us -> 5.52 us
  transfers between devices with their start and end apart: 4 -> 4, of which waited for: 3 -> 3; matrix products, arithmetic and copies ran while one was open for 29% -> 26% of each run, Pallas kernels for 0% -> 0%
where the time goes in v1:
time: 239 us; the launch traced here: 238 us
  waiting for transfers between devices  116 us (49%)
  local copies, waits for them, and re-layouts  38.7 us (16%)
  matrix products  35.3 us (15%)
  starting transfers between devices  22.3 us (9%)
  between operations  14.3 us (6%)
  other arithmetic  11.5 us (5%)
    reduce_scatter x1, waiting for transfers between devices, body(): lax.psum_scatter(projected_rows(jnp.int32(0), mode_count, 0), 'leaf', sca...  71.5 us
    all_to_all x1, waiting for transfers between devices, pack_results(): lax.all_to_all(jnp.stack([base_x] * lax.axis_size(mesh_ax), 0), axis_name...  44.2 us
    convert_element_type x2, local copies, waits for them, and re-layouts, body(): sides = placed[leaf_order:].astype(jnp.float32)  13.2 us
    all_to_all x1, starting transfers between devices, body(): lax.all_to_all(root_rows.reshape(device_count, root_width // device_count...  12.5 us
    all_to_all x1, starting transfers between devices, pack_results(): lax.all_to_all(jnp.stack([base_x] * lax.axis_size(mesh_ax), 0), axis_name...  9.76 us
    concatenate x3, local copies, waits for them, and re-layouts, body(): jnp.concatenate([leaf_modes[0], mass_coupling[0], damp_coupling[0]], axis=0)  9.02 us
    dot_general x6, matrix products, left_product(): lax.dot_general(first_operand, second_operand, (((0,), (0,)), ((), ())),...  7.12 us
    dot_general x1, matrix products, body(): jnp.dot(half_work, mode_basis, preferred_element_type=jnp.float32)  6.74 us
  transfers between devices with their start and end apart: 4, of which 3 were waited for; matrix products, arithmetic and copies ran while one was open for 26% of the time, Pallas kernels for 0%

profile of v1, /device:TPU:4, one launch (start us, length us, event | category | flops | bytes accessed | tf_op | source)
XLA Modules:
  0.0 238.1 jit_solution(16512868729608290500)
XLA Ops:
  7.2 0.9 pad_maximum_fusion.8
  8.1 2.2 stack.2
  10.4 9.8 %all-to-all-start = ((bf16[16,96,1280]{2,1,0:T(8,128)(2,1)}), bf16[16,96,1280]{2,1,0:T(8,128)(2,1)}, u32[]{:S(2)}, u32[]{:S(2)}) async-start(bf16[16,96,1280]{2,1,0:T(8,128)(2,1)} %stack.2), calls=%async_computation | async-start | bytes 7864320 | tf_op jit(solution)/shard_map/all_to_all | solution.py:10
  20.1 0.0 reduce-scatter.2.cloned.1.call-start
  20.2 0.7 copy.26
  20.9 0.0 copy-start.3
  20.9 3.0 %copy.29 = bf16[512,12,128]{2,1,0:T(8,128)(2,1)} copy(bf16[512,12,128]{0,2,1:T(8,128)(2,1)S(1)} %bitcast.43) | data formatting | bytes 3145728 | tf_op jit(solution)/shard_map/concatenate | solution.py:63
  23.9 0.7 copy.25
  24.7 0.0 copy-start.4
  24.7 3.0 %copy.28 = bf16[512,12,128]{2,1,0:T(8,128)(2,1)} copy(bf16[512,12,128]{0,2,1:T(8,128)(2,1)S(1)} %bitcast.44) | data formatting | bytes 3145728 | tf_op jit(solution)/shard_map/concatenate | solution.py:63
  27.7 0.7 copy.24
  28.4 0.0 copy-start.8
  28.4 3.0 %copy.27 = bf16[512,12,128]{2,1,0:T(8,128)(2,1)} copy(bf16[512,12,128]{0,2,1:T(8,128)(2,1)S(1)} %bitcast.45) | data formatting | bytes 3145728 | tf_op jit(solution)/shard_map/concatenate | solution.py:63
  31.4 4.6 %fusion = bf16[12,1536,128]{2,0,1:T(8,128)(2,1)S(1)} fusion(bf16[512,12,128]{2,1,0:T(8,128)(2,1)} %copy.29, bf16[512,12,128]{2,1,0:T(8,128)(2,1)} %copy.28, bf16[512,12,128]{2,1,0:T(8,128)(2,1)} %copy.27, s32[12]{0:T(128)S(1)} %bitcast.52), kind=kOutput, calls=%fused_computation.1 | convolution fusion | flops 70779024 | bytes 9437232 | tf_op jit(solution)/shard_map/lbk,bj->ljk/dot_general | solution.py:25
  36.0 1.2 copy.38
  37.3 2.2 copy-done
  39.5 0.1 slice.81
  39.6 1.6 copy.31
  41.2 5.1 %slice_convert_fusion = f32[1024,12,128]{2,0,1:T(8,128)} fusion(bf16[1536,12,128]{2,0,1:T(8,128)(2,1)} %bitcast.41), kind=kLoop, calls=%fused_computation.14 | loop fusion | flops 1572864 | bytes 9437184 | tf_op jit(solution)/shard_map/convert_element_type | solution.py:69
  46.3 6.6 %copy.32 = f32[1024,12,128]{0,2,1:T(8,128)} copy(f32[1024,12,128]{2,0,1:T(8,128)} %slice_convert_fusion) | data formatting | bytes 12582912 | tf_op jit(solution)/shard_map/convert_element_type | solution.py:69
  52.9 6.7 %copy.33 = f32[1024,1536]{1,0:T(8,128)} copy(f32[1024,1536]{0,1:T(8,128)} %bitcast.39) | data formatting | bytes 12582912 | tf_op jit(solution)/shard_map/convert_element_type | solution.py:69
  59.6 6.0 %fusion.14 = f32[1024,1536]{1,0:T(8,128)} fusion(bf16[512,1536]{0,1:T(8,128)(2,1)} %bitcast.46, bf16[512,512]{1,0:T(8,128)(2,1)S(1)} %bitcast.50, bf16[512,512]{1,0:T(8,128)(2,1)S(1)} %bitcast.51), kind=kOutput, calls=%fused_computation.28 | convolution fusion | flops 1612709888 | bytes 8912896 | tf_op jit(solution)/shard_map/dot_general | solution.py:70
  65.6 44.2 %all-to-all-done = bf16[16,96,1280]{2,1,0:T(8,128)(2,1)} async-done(((bf16[16,96,1280]{2,1,0:T(8,128)(2,1)}), bf16[16,96,1280]{2,1,0:T(8,128)(2,1)}, u32[]{:S(2)}, u32[]{:S(2)}) %all-to-all-start) | async-done | bytes 3932192 | tf_op jit(solution)/shard_map/all_to_all | solution.py:10
  109.7 5.0 %convolution_convert_fusion.1 = bf16[512,1280]{1,0:T(8,128)(2,1)S(1)} fusion(bf16[512,1536]{0,1:T(8,128)(2,1)} %bitcast.47, bf16[1536,1280]{1,0:T(8,128)(2,1)} %bitcast.12), kind=kOutput, calls=%fused_computation.16 | convolution fusion | flops 2013921280 | bytes 6815744 | tf_op jit(solution)/shard_map/dot_general | solution.py:79
  114.7 0.1 slice.92
  114.9 0.5 copy-done.1
  115.4 6.7 %convolution_convert_fusion = bf16[1024,1280]{1,0:T(8,128)(2,1)S(1)} fusion(bf16[1536,1280]{1,0:T(8,128)(2,1)} %bitcast.12, f32[1024,1536]{1,0:T(8,128)S(1)} %bitcast.38, f32[1024,1536]{1,0:T(8,128)S(1)} %copy-done.1), kind=kOutput, calls=%fused_computation.12 | convolution fusion | flops 4032561152 | bytes 19136512 | tf_op jit(solution)/shard_map/dot_general | solution.py:80
  122.2 1.2 broadcast_select_fusion
  123.3 1.6 pad_maximum_fusion.1
  124.9 0.5 fusion.10
  125.5 0.5 fusion.12
  126.0 0.5 convolution_add_fusion
  126.5 0.5 convolution_add_fusion.1
  127.1 1.8 pad_maximum_fusion
  128.9 0.0 reduce-scatter.2.cloned.1.call-update
  128.9 0.4 collective-permute-done
  129.3 0.2 fusion.31
  129.5 0.6 copy-done.5
  130.1 2.4 %fusion.9 = f32[1024,1024]{1,0:T(8,128)S(1)} fusion(bf16[512,1024]{1,0:T(8,128)(2,1)S(1)} %get-tuple-element.9, bf16[512,1024]{1,0:T(8,128)(2,1)S(1)} %copy-done.5, bf16[512,1024]{1,0:T(8,128)(2,1)S(1)} %slice.92, bf16[512,1024]{1,0:T(8,128)(2,1)S(1)} %get-tuple-element.8), kind=kOutput, calls=%fused_computation.23 | convolution fusion | flops 2155872256 | bytes 8388608 | tf_op jit(solution)/shard_map/dot_general | solution.py:35
  132.5 2.6 %add_convert_fusion.2 = bf16[1024,1024]{1,0:T(8,128)(2,1)S(1)} fusion(f32[1024,1024]{1,0:T(8,128)S(1)} %fusion.9, bf16[512,1024]{1,0:T(8,128)(2,1)S(1)} %get-tuple-element.9, bf16[512,1024]{1,0:T(8,128)(2,1)S(1)} %copy-done.5, bf16[512,1024]{1,0:T(8,128)(2,1)S(1)} %slice.92, bf16[512,1024]{1,0:T(8,128)(2,1)S(1)} %get-tuple-element.8), kind=kOutput, calls=%fused_computation.11 | convolution fusion | flops 2157969408 | bytes 10485760 | tf_op jit(solution)/shard_map/dot_general | solution.py:35
  135.1 2.2 convert_element_type.46
  137.4 12.5 %all-to-all-start.1 = ((bf16[256,4,1024]{2,1,0:T(4,128)(2,1)}), bf16[256,4,1024]{2,1,0:T(4,128)(2,1)S(1)}, u32[]{:S(2)}, u32[]{:S(2)}) async-start(bf16[256,4,1024]{2,1,0:T(4,128)(2,1)} %convert_element_type.46), calls=%async_computation.2 | async-start | bytes 4194304 | tf_op jit(solution)/shard_map/all_to_all | solution.py:117
  149.8 5.8 %fusion.7 = f32[1024,256]{1,0:T(8,128)S(1)} fusion(f32[1024,1536]{1,0:T(8,128)} %fusion.14, f32[1024,1536]{1,0:T(8,128)} %copy.33, bf16[1536,1280]{1,0:T(8,128)(2,1)} %bitcast.12), kind=kOutput, calls=%fused_computation.13 | convolution fusion | flops 808452096 | bytes 14417920 | tf_op jit(solution)/shard_map/dot_general | solution.py:81
  155.7 1.0 slice_bitcast_fusion
  156.7 71.5 %reduce-scatter.2.cloned.1.call-done = f32[16,2560]{1,0:T(8,128)} async-done(((f32[256,2560]{1,0:T(8,128)}), f32[16,2560]{1,0:T(8,128)}) %reduce-scatter.2.cloned.1.call-update) | async-done | bytes 163856 | tf_op jit(solution)/shard_map/reduce_scatter | solution.py:99
  228.2 1.6 slice_bitcast_fusion.2
  229.8 0.8 convert_reduce_fusion
  230.7 0.6 slice_bitcast_fusion.4
  (19 shorter events, 0.0 us)
Async XLA Ops:
  10.4 9.8 %copy-start.2 = (bf16[1,512,1536]{2,1,0:T(8,128)(2,1)S(1)}, bf16[1,512,1536]{2,1,0:T(8,128)(2,1)}, u32[]{:S(2)}) copy-start(bf16[1,512,1536]{2,1,0:T(8,128)(2,1)} %param.11) | copy-start | bytes 4718596
  10.4 99.4 %all-to-all-start = ((bf16[16,96,1280]{2,1,0:T(8,128)(2,1)}), bf16[16,96,1280]{2,1,0:T(8,128)(2,1)}, u32[]{:S(2)}, u32[]{:S(2)}) async-start(bf16[16,96,1280]{2,1,0:T(8,128)(2,1)} %stack.2), calls=%async_computation | async-start | bytes 7864320 | tf_op jit(solution)/shard_map/all_to_all | solution.py:10
  20.1 208.1 %reduce-scatter.2.cloned.1.call-start = ((), (), s32[]{:S(2)}) async-start(), calls=%async_computation.3 | async-start | bytes 2785280 | tf_op jit(solution)/shard_map/reduce_scatter | solution.py:99
  20.9 3.0 %copy-start.3 = (bf16[1,512,1536]{2,1,0:T(8,128)(2,1)S(1)}, bf16[1,512,1536]{2,1,0:T(8,128)(2,1)}, u32[]{:S(2)}) copy-start(bf16[1,512,1536]{2,1,0:T(8,128)(2,1)} %param.10) | copy-start | bytes 4718596
  24.7 3.0 %copy-start.4 = (bf16[1,512,1536]{2,1,0:T(8,128)(2,1)S(1)}, bf16[1,512,1536]{2,1,0:T(8,128)(2,1)}, u32[]{:S(2)}) copy-start(bf16[1,512,1536]{2,1,0:T(8,128)(2,1)} %param.12) | copy-start | bytes 4718596
  28.4 3.0 %copy-start.8 = (s32[1,12]{1,0:T(1,128)S(1)}, s32[1,12]{1,0:T(1,128)}, u32[]{:S(2)}) copy-start(s32[1,12]{1,0:T(1,128)} %param.13) | copy-start | bytes 148
  37.3 2.2 copy-start
  52.9 6.7 %copy-start.6 = (bf16[1,512,512]{2,1,0:T(8,128)(2,1)S(1)}, bf16[1,512,512]{2,1,0:T(8,128)(2,1)}, u32[]{:S(2)}) copy-start(bf16[1,512,512]{2,1,0:T(8,128)(2,1)} %param.9) | copy-start | bytes 1572868
  52.9 6.7 %copy-start.7 = (bf16[1,512,512]{2,1,0:T(8,128)(2,1)S(1)}, bf16[1,512,512]{2,1,0:T(8,128)(2,1)}, u32[]{:S(2)}) copy-start(bf16[1,512,512]{2,1,0:T(8,128)(2,1)} %param.8) | copy-start | bytes 1572868
  59.6 55.3 %slice-start = ((s8[6291456]{0:T(1024)(128)(4,1)}), s8[2097152]{0:T(1024)(128)(4,1)S(1)}, s32[]{:S(2)}) async-start(s8[6291456]{0:T(1024)(128)(4,1)} %bitcast.37), calls=%async_computation.4 | async-start | bytes 4194304
  109.7 5.2 %slice-start.1 = ((s8[6291456]{0:T(1024)(128)(4,1)}), s8[4194304]{0:T(1024)(128)(4,1)S(1)}, s32[]{:S(2)}) async-start(s8[6291456]{0:T(1024)(128)(4,1)} %bitcast.37), calls=%async_computation.5 | async-start | bytes 8388608
  109.7 5.7 %copy-start.1 = (f32[1024,1536]{1,0:T(8,128)S(1)}, f32[1024,1536]{1,0:T(8,128)}, u32[]{:S(2)}) copy-start(f32[1024,1536]{1,0:T(8,128)} %fusion.14) | copy-start | bytes 18874372
  124.9 4.4 %collective-permute-start = (bf16[1024,1024]{1,0:T(8,128)(2,1)}, bf16[1024,1024]{1,0:T(8,128)(2,1)S(1)}, u32[]{:S(2)}, u32[]{:S(2)}) collective-permute-start(bf16[1024,1024]{1,0:T(8,128)(2,1)} %pad_maximum_fusion.1), channel_id=1, source_target_pairs={{0,16},{16,0},{32,48},{48,32},{64,80},{80,64},{96,112},{112,96},{1... | collective-permute-start | bytes 6291464 | tf_op jit(solution)/shard_map/ppermute | solution.py:109
  128.9 1.2 copy-start.5
  137.4 92.4 %all-to-all-start.1 = ((bf16[256,4,1024]{2,1,0:T(4,128)(2,1)}), bf16[256,4,1024]{2,1,0:T(4,128)(2,1)S(1)}, u32[]{:S(2)}, u32[]{:S(2)}) async-start(bf16[256,4,1024]{2,1,0:T(4,128)(2,1)} %convert_element_type.46), calls=%async_computation.2 | async-start | bytes 4194304 | tf_op jit(solution)/shard_map/all_to_all | solution.py:117
Sparse Core Ops, SparseCore 0:
  129.0 99.1 reduce-scatter.1
